TPU v7x, 128 devices: a whole 4x4x4 slice. The times are simulated.
128 devices in a mesh: req: 16 (over y, z), mp: 8 (over x, core).
Axes of the slice: x: 4, y: 4, z: 4, core: 2. Of those that a mesh axis runs over, the one named last changes fastest.
Arguments:
- hidden_in: bfloat16 [16384, 2048], P('req', 'mp'), may hold values from -6 to 6
- w_qkv: bfloat16 [3, 2048, 2048], P(None, 'req', 'mp'), may hold values from -0.125 to 0.125
- w_out: bfloat16 [2048, 2048], P('mp', 'req'), may hold values from -0.125 to 0.125
- attn_gain: bfloat16 [2048], replicated, may hold values from 0.099609375 to 1.8984375
- mlp_gain: bfloat16 [2048], replicated, may hold values from 0.099609375 to 1.8984375
- w_gate: bfloat16 [2048, 8192], P('req', 'mp'), may hold values from -0.125 to 0.125
- w_up: bfloat16 [2048, 8192], P('req', 'mp'), may hold values from -0.125 to 0.125
- w_down: bfloat16 [8192, 2048], P('mp', 'req'), may hold values from -0.0625 to 0.0625
- k_cache: bfloat16 [16, 4096, 2048], P('req', None, 'mp'), may hold values from -363 to 363
- v_cache: bfloat16 [16, 4096, 2048], P('req', None, 'mp'), may hold values from -6 to 6
- cache_len: int32 [16], P('req'), may hold values from 256 to 4096, as said below
Outputs:
- hidden_out: bfloat16 [16384, 2048], P('req', 'mp')
- new_keys: bfloat16 [16384, 2048], P('req', 'mp')
- new_values: bfloat16 [16384, 2048], P('req', 'mp')
Inputs may be any that keep to these rules, and one draw needn't show every extreme that they name: Each request uses its first cache_len slots; later slots hold unused data. Some request's cache is full in every draw.
All inputs are finite; a program needn't handle non-finite values.
Results may differ from a plain program's by a relative error of at most 0.02.
Values may be sent and summed in bfloat16 or wider, within the bound.
No kernel may reach another device: no remote copies, remote signals or barrier semaphores. Data moves between devices by JAX's collectives and lax.ppermute only.
A program may use at most 128 MiB of HBM per device.

v0:
```python
import jax
import jax.numpy as jnp
from jax import lax
from jax.sharding import PartitionSpec as P

HD = 64
THETA = 130000.0
EPSILON = 1e-05
NEG_FILL = -1e30


def rms_scale(rows, gain):
    values = rows.astype(jnp.float32)
    meansq = jnp.mean(values * values, axis=-1, keepdims=True)
    return (values * lax.rsqrt(meansq + EPSILON) * gain.astype(jnp.float32)).astype(jnp.bfloat16)


def rotate(tensor, positions):
    half = tensor.shape[-1] // 2
    freq = THETA ** (-(jnp.arange(half, dtype=jnp.float32) * 2.0 / tensor.shape[-1]))
    angle = positions[:, None, None] * freq[None, None, :]
    cosine = jnp.cos(angle)
    sine = jnp.sin(angle)
    first = tensor[..., :half]
    second = tensor[..., half:]
    return jnp.concatenate(
        [first * cosine - second * sine, second * cosine + first * sine], axis=-1
    )


def absorb(carry, queries, keys, values, valid):
    top, total, accum = carry
    scores = jnp.einsum("qhd,khd->hqk", queries, keys, preferred_element_type=jnp.float32) * HD ** (
        -0.5
    )
    scores = jnp.where(valid[None], scores, NEG_FILL)
    new_top = jnp.maximum(top, jnp.max(scores, axis=-1, keepdims=True))
    factor = jnp.exp(top - new_top)
    probs = jnp.where(valid[None], jnp.exp(scores - new_top), 0.0)
    total = total * factor + jnp.sum(probs, axis=-1, keepdims=True)
    accum = accum * factor + jnp.einsum(
        "hqk,khd->hqd", probs.astype(jnp.bfloat16), values, preferred_element_type=jnp.float32
    )
    return (new_top, total, accum)


def on_device(
    hidden_in, w_qkv, w_out, attn_gain, mlp_gain, w_gate, w_up, w_down, k_cache, v_cache, cache_len
):
    new_count = hidden_in.shape[0]
    width = w_qkv.shape[2]
    heads_local = width // HD
    slots = k_cache.shape[1]
    full_rows = lax.all_gather(hidden_in, "mp", axis=1, tiled=True)
    normed = rms_scale(full_rows, attn_gain)
    columns = normed
    projected = jnp.einsum(
        "nd,kdw->knw",
        columns,
        lax.all_gather(w_qkv, "req", axis=1, tiled=True),
        preferred_element_type=jnp.float32,
    )
    length = cache_len[0]
    positions = (length + jnp.arange(new_count, dtype=jnp.int32)).astype(jnp.float32)
    queries = rotate(projected[0].reshape(new_count, heads_local, HD), positions).astype(
        jnp.bfloat16
    )
    fresh_keys = rotate(projected[1].reshape(new_count, heads_local, HD), positions).astype(
        jnp.bfloat16
    )
    fresh_values = projected[2].astype(jnp.bfloat16).reshape(new_count, heads_local, HD)
    rows = jnp.arange(new_count, dtype=jnp.int32)
    causal = rows[:, None] >= rows[None, :]
    start_carry = (
        jnp.full((heads_local, new_count, 1), NEG_FILL, jnp.float32),
        jnp.zeros((heads_local, new_count, 1), jnp.float32),
        jnp.zeros((heads_local, new_count, HD), jnp.float32),
    )
    carry = absorb(start_carry, queries, fresh_keys, fresh_values, causal)
    cache_keys = k_cache[0].reshape(slots, heads_local, HD)
    cache_values = v_cache[0].reshape(slots, heads_local, HD)
    block = min(slots, 512)
    count = (length + block - 1) // block

    def step_block(index, state):
        begin = index * block
        keys = lax.dynamic_slice_in_dim(cache_keys, begin, block, 0)
        values = lax.dynamic_slice_in_dim(cache_values, begin, block, 0)
        valid = (begin + jnp.arange(block, dtype=jnp.int32) < length)[None, :]
        return absorb(state, queries, keys, values, valid)

    top, total, accum = lax.fori_loop(0, count, step_block, carry)
    attn = (accum / total).transpose(1, 0, 2).reshape(new_count, width).astype(jnp.bfloat16)
    partial_value = jnp.dot(
        attn, lax.all_gather(w_out, "req", axis=1, tiled=True), preferred_element_type=jnp.float32
    )
    summed = lax.psum_scatter(
        partial_value.astype(jnp.bfloat16), "mp", scatter_dimension=1, tiled=True
    ).astype(jnp.float32)
    mid_local = (hidden_in.astype(jnp.float32) + summed).astype(jnp.bfloat16)
    mid_full = lax.all_gather(mid_local, "mp", axis=1, tiled=True)
    normed2 = rms_scale(mid_full, mlp_gain)
    columns = normed2
    gate = jnp.dot(
        columns,
        lax.all_gather(w_gate, "req", axis=0, tiled=True),
        preferred_element_type=jnp.float32,
    )
    upper = jnp.dot(
        columns, lax.all_gather(w_up, "req", axis=0, tiled=True), preferred_element_type=jnp.float32
    )
    units = (jax.nn.silu(gate) * upper).astype(jnp.bfloat16)
    terms = jnp.dot(
        units, lax.all_gather(w_down, "req", axis=1, tiled=True), preferred_element_type=jnp.float32
    )
    reduced = lax.psum_scatter(
        terms.astype(jnp.bfloat16), "mp", scatter_dimension=1, tiled=True
    ).astype(jnp.float32)
    hidden_out = (mid_local.astype(jnp.float32) + reduced).astype(jnp.bfloat16)
    return (
        hidden_out,
        fresh_keys.reshape(new_count, width),
        fresh_values.reshape(new_count, width),
    )


def solution(mesh):
    return jax.shard_map(
        on_device,
        mesh=mesh,
        in_specs=(
            P("req", "mp"),
            P(None, "req", "mp"),
            P("mp", "req"),
            P(),
            P(),
            P("req", "mp"),
            P("req", "mp"),
            P("mp", "req"),
            P("req", None, "mp"),
            P("req", None, "mp"),
            P("req"),
        ),
        out_specs=(P("req", "mp"), P("req", "mp"), P("req", "mp")),
        check_vma=False,
    )
```

profile of v0, /device:TPU:0, one launch (start us, length us, event | category | flops | bytes accessed | tf_op | source)
XLA Modules:
  0.0 499.0 jit_solution(9587442802145398446)
XLA Ops:
  7.2 0.0 all-gather.8.cloned.1.call-start
  7.2 0.7 all-gather.8.cloned.1.call-update
  7.9 0.0 all-gather.10.cloned.1.call-start
  7.9 1.7 copy.15
  9.7 0.0 all-gather.10.cloned.1.call-update
  9.7 0.0 all-gather.12.cloned.1.call-start
  9.8 0.7 all-gather.12.cloned.1.call-update
  10.4 0.0 reduce-scatter.3.cloned.1.call-start
  10.5 1.3 iota_compare_fusion
  12.4 0.7 convert_element_type.87
  13.1 2.9 copy.17
  16.1 4.2 copy.18
  20.2 0.5 multiply_cosine_fusion
  20.8 27.4 %all-gather.8.cloned.1.call-done = bf16[1024,2048]{1,0:T(8,128)(2,1)} async-done(((bf16[1024,256]{1,0:T(8,128)(2,1)}), bf16[1024,2048]{1,0:T(8,128)(2,1)}) %all-gather.8.cloned.1.call-update) | async-done | bytes 4194320 | tf_op jit(solution)/shard_map/all_gather | solution.py:54
  48.2 3.1 fusion.23
  51.3 53.4 %all-gather.10.cloned.1.call-done = bf16[3,2048,256]{1,2,0:T(8,128)(2,1)} async-done(((bf16[3,128,256]{1,2,0:T(8,128)(2,1)}), bf16[3,2048,256]{1,2,0:T(8,128)(2,1)}) %all-gather.10.cloned.1.call-update) | async-done | bytes 3145744 | tf_op jit(solution)/shard_map/all_gather | solution.py:60
  104.7 6.6 %fusion.37 = f32[3,1024,256]{1,2,0:T(8,128)S(1)} fusion(bf16[3,2048,256]{1,2,0:T(8,128)(2,1)} %all-gather.10.cloned.1.call-done, bf16[1024,2048]{1,0:T(8,128)(2,1)} %all-gather.8.cloned.1.call-done, f32[2048]{0:T(1024)S(1)} %convert_element_type.87, f32[1024]{0:T(1024)S(1)} %add_rsqrt_fusion.1), kind=kOutput, calls=%fused_computation.49 | convolution fusion | flops 3229614080 | bytes 10498048 | tf_op jit(solution)/shard_map/nd,kdw->knw/dot_general | solution.py:57
  111.3 0.0 copy-start.2
  111.3 0.0 copy-start.1
  111.3 0.2 fusion.54
  111.6 0.1 slice.44
  111.6 0.2 subtract_convert_fusion
  111.8 0.2 multiply_subtract_fusion
  112.0 1.0 copy-done.2
  113.0 0.3 copy-done.1
  113.3 3.0 fusion.20
  116.4 4.2 fusion.22
  120.6 5.9 %fusion.40 = f32[4,1024,64]{1,2,0:T(8,128)} fusion(bf16[1024,4,64]{0,2,1:T(8,128)(2,1)S(1)} %bitcast.80, f32[4,1024,1024]{1,2,0:T(8,128)S(1)} %get-tuple-element.91, f32[4,1024]{1,0:T(4,128)S(1)} %get-tuple-element.87, pred[1024,1024]{0,1:T(8,128)(4,1)S(1)} %copy-done.1, f32[4,1024]{1,0:T(4,128)S(1)} %get-tuple-element.85), kind=kOutput, calls=%fused_computation.50 | convolution fusion | flops 558104576 | bytes 19431424 | tf_op jit(solution)/shard_map/hqk,khd->hqd/dot_general | solution.py:41
  126.5 8.1 %while.14 = (s32[]{:T(128)}, f32[4,1024,1]{1,0,2:T(4,128)S(1)}, f32[4,1024,1]{1,0,2:T(4,128)S(1)}, f32[4,1024,64]{1,2,0:T(8,128)}, s32[]{:T(128)}, /*index=5*/s3...) while((s32[]{:T(128)}, f32[4,1024,1]{1,0,2:T(4,128)S(1)}, ...), condition=%wide.region_6.7_spmd, body=%wide.region_3.6_spmd.sunk | while | flops 564671488 | bytes 36965104 | solution.py:92
  126.5 0.7 add_compare_fusion.2
  127.3 1.6 bitcast_reduce_fusion.2
  128.9 3.1 fusion.74
  132.0 0.0 copy-start.5
  132.0 2.5 fusion.73
  134.6 0.0 copy-start.3
  134.6 0.0 copy-start.6
  134.6 1.4 divide_convert_fusion
  136.0 13.5 %all-gather.12.cloned.1.call-done = bf16[256,2048]{1,0:T(8,128)(2,1)} async-done(((bf16[256,128]{1,0:T(8,128)(2,1)}), bf16[256,2048]{1,0:T(8,128)(2,1)}) %all-gather.12.cloned.1.call-update) | async-done | bytes 1048592 | tf_op jit(solution)/shard_map/all_gather | solution.py:95
  149.5 4.5 convolution_convert_fusion
  154.0 0.0 reduce-scatter.3.cloned.1.call-update
  154.0 0.0 all-gather.14.cloned.1.call-start
  154.1 79.0 %reduce-scatter.3.cloned.1.call-done = bf16[1024,256]{1,0:T(8,128)(2,1)} async-done(((bf16[1024,2048]{1,0:T(8,128)(2,1)}), bf16[1024,256]{1,0:T(8,128)(2,1)}) %reduce-scatter.3.cloned.1.call-update) | async-done | bytes 524304 | tf_op jit(solution)/shard_map/reduce_scatter | solution.py:97
  233.1 2.0 add_convert_fusion.1
  235.1 0.0 all-gather.14.cloned.1.call-update
  235.1 0.0 all-gather.16.cloned.1.call-start
  235.2 0.5 all-gather.16.cloned.1.call-update
  235.7 0.0 all-gather.18.cloned.1.call-start
  235.7 0.7 all-gather.18.cloned.1.call-update
  236.4 0.0 all-gather.20.cloned.1.call-start
  236.5 0.7 all-gather.20.cloned.1.call-update
  237.2 0.3 reduce-scatter.5.cloned.1.call-start
  237.5 32.8 %all-gather.14.cloned.1.call-done = bf16[1024,2048]{1,0:T(8,128)(2,1)} async-done(((bf16[1024,256]{1,0:T(8,128)(2,1)}), bf16[1024,2048]{1,0:T(8,128)(2,1)}) %all-gather.14.cloned.1.call-update) | async-done | bytes 4194320 | tf_op jit(solution)/shard_map/all_gather | solution.py:101
  270.3 3.1 fusion.26
  273.4 51.6 %all-gather.16.cloned.1.call-done = bf16[2048,1024]{1,0:T(8,128)(2,1)} async-done(((bf16[128,1024]{1,0:T(8,128)(2,1)}), bf16[2048,1024]{1,0:T(8,128)(2,1)}) %all-gather.16.cloned.1.call-update) | async-done | bytes 4194320 | tf_op jit(solution)/shard_map/all_gather | solution.py:106
  325.0 10.0 %fusion.44 = f32[1024,1024]{1,0:T(8,128)} fusion(bf16[2048,1024]{1,0:T(8,128)(2,1)} %all-gather.16.cloned.1.call-done, bf16[1024,2048]{1,0:T(8,128)(2,1)} %all-gather.14.cloned.1.call-done, f32[2048]{0:T(1024)S(1)} %convert_element_type.102, f32[1024]{0:T(1024)S(1)} %add_rsqrt_fusion), kind=kOutput, calls=%fused_computation.51 | convolution fusion | flops 4303355904 | bytes 12595200 | tf_op jit(solution)/shard_map/dot_general | solution.py:104
  335.0 43.5 %all-gather.18.cloned.1.call-done = bf16[2048,1024]{1,0:T(8,128)(2,1)} async-done(((bf16[128,1024]{1,0:T(8,128)(2,1)}), bf16[2048,1024]{1,0:T(8,128)(2,1)}) %all-gather.18.cloned.1.call-update) | async-done | bytes 4194320 | tf_op jit(solution)/shard_map/all_gather | solution.py:110
  378.4 59.4 %all-gather.20.cloned.1.call-done = bf16[1024,2048]{1,0:T(8,128)(2,1)} async-done(((bf16[1024,128]{1,0:T(8,128)(2,1)}), bf16[1024,2048]{1,0:T(8,128)(2,1)}) %all-gather.20.cloned.1.call-update) | async-done | bytes 4194320 | tf_op jit(solution)/shard_map/all_gather | solution.py:114
  437.9 15.4 %convolution_convert_fusion.1 = bf16[1024,2048]{1,0:T(8,128)(2,1)} fusion(bf16[1024,2048]{1,0:T(8,128)(2,1)} %all-gather.20.cloned.1.call-done, f32[1024,1024]{1,0:T(8,128)} %fusion.44, bf16[2048,1024]{1,0:T(8,128)(2,1)} %all-gather.18.cloned.1.call-done, bf16[1024,2048]{1,0:T(8,128)(2,1)} %all-gather.14.cloned.1.call-done, ...), kind=kOutput, calls=%fused_computation.48 | convolution fusion | flops 8606711808 | bytes 20983808 | tf_op jit(solution)/shard_map/dot_general | solution.py:113
  453.3 0.0 reduce-scatter.5.cloned.1.call-update
  453.3 1.0 copy.19
  454.3 1.3 slice_bitcast_fusion
  455.6 1.0 copy.20
  456.6 33.9 %reduce-scatter.5.cloned.1.call-done = bf16[1024,256]{1,0:T(8,128)(2,1)} async-done(((bf16[1024,2048]{1,0:T(8,128)(2,1)}), bf16[1024,256]{1,0:T(8,128)(2,1)}) %reduce-scatter.5.cloned.1.call-update) | async-done | bytes 524304 | tf_op jit(solution)/shard_map/reduce_scatter | solution.py:116
  490.5 2.0 add_convert_fusion
  (19 shorter events, 0.2 us)
Async XLA Ops:
  7.2 41.0 %all-gather.8.cloned.1.call-start = ((), (), s32[]{:S(2)}) async-start(), calls=%async_computation.2 | async-start | bytes 4718592 | tf_op jit(solution)/shard_map/all_gather | solution.py:54
  7.9 96.8 %all-gather.10.cloned.1.call-start = ((), (), s32[]{:S(2)}) async-start(), calls=%async_computation.3 | async-start | bytes 3342336 | tf_op jit(solution)/shard_map/all_gather | solution.py:60
  9.7 139.8 %all-gather.12.cloned.1.call-start = ((), (), s32[]{:S(2)}) async-start(), calls=%async_computation.4 | async-start | bytes 1114112 | tf_op jit(solution)/shard_map/all_gather | solution.py:95
  10.4 222.7 %reduce-scatter.3.cloned.1.call-start = ((), (), s32[]{:S(2)}) async-start(), calls=%async_computation.5 | async-start | bytes 4718592 | tf_op jit(solution)/shard_map/reduce_scatter | solution.py:97
  111.3 1.7 copy-start.2
  111.3 2.0 copy-start.1
  126.5 2.4 copy-start.4
  132.0 2.6 copy-start.5
  134.6 98.5 %copy-start.3 = (bf16[1024,256]{1,0:T(8,128)(2,1)S(1)}, bf16[1024,256]{1,0:T(8,128)(2,1)}, u32[]{:S(2)}) copy-start(bf16[1024,256]{1,0:T(8,128)(2,1)} %param.13) | copy-start | bytes 1572868
  134.6 102.9 %copy-start.6 = (bf16[2048]{0:T(1024)(128)(2,1)S(1)}, bf16[2048]{0:T(1024)(128)(2,1)}, u32[]{:S(2)}) copy-start(bf16[2048]{0:T(1024)(128)(2,1)} %param.17) | copy-start | bytes 12292
  154.0 116.3 %all-gather.14.cloned.1.call-start = ((), (), s32[]{:S(2)}) async-start(), calls=%async_computation.6 | async-start | bytes 4718592 | tf_op jit(solution)/shard_map/all_gather | solution.py:101
  235.1 89.9 %all-gather.16.cloned.1.call-start = ((), (), s32[]{:S(2)}) async-start(), calls=%async_computation.7 | async-start | bytes 4456448 | tf_op jit(solution)/shard_map/all_gather | solution.py:106
  235.7 142.7 %all-gather.18.cloned.1.call-start = ((), (), s32[]{:S(2)}) async-start(), calls=%async_computation.8 | async-start | bytes 4456448 | tf_op jit(solution)/shard_map/all_gather | solution.py:110
  236.4 201.4 %all-gather.20.cloned.1.call-start = ((), (), s32[]{:S(2)}) async-start(), calls=%async_computation.9 | async-start | bytes 4456448 | tf_op jit(solution)/shard_map/all_gather | solution.py:114
  237.2 253.3 %reduce-scatter.5.cloned.1.call-start = ((), (), s32[]{:S(2)}) async-start(), calls=%async_computation.10 | async-start | bytes 4718592 | tf_op jit(solution)/shard_map/reduce_scatter | solution.py:116
  453.3 37.2 %copy-start = (bf16[1024,256]{1,0:T(8,128)(2,1)S(1)}, bf16[1024,256]{1,0:T(8,128)(2,1)}, u32[]{:S(2)}) copy-start(bf16[1024,256]{1,0:T(8,128)(2,1)} %add_convert_fusion.1) | copy-start | bytes 1572868
Sparse Core Ops, SparseCore 0:
  9.7 38.4 all-gather.7
  50.9 53.7 all-gather.9
  106.8 42.7 all-gather.11
  154.2 78.9 reduce-scatter.2
  235.2 35.0 all-gather.13
  272.3 52.6 all-gather.15
  327.2 51.2 all-gather.17
  380.5 57.2 all-gather.19
  453.4 37.0 reduce-scatter.4
where the time goes:
time: 500 us; the launch traced here: 499 us
  waiting for transfers between devices  398 us (80%)
  matrix products  50 us (10%)
  other arithmetic  21.9 us (4%)
  between operations  14.7 us (3%)
  local copies, waits for them, and re-layouts  13.8 us (3%)
    reduce_scatter x1, waiting for transfers between devices, on_device(): lax.psum_scatter(partial_value.astype(jnp.bfloat16), 'mp', scatter_dimens...  79 us
    all_gather x1, waiting for transfers between devices, on_device(): lax.all_gather(w_down, 'req', axis=1, tiled=True)  59.4 us
    all_gather x1, waiting for transfers between devices, on_device(): lax.all_gather(w_qkv, 'req', axis=1, tiled=True)  53.4 us
    all_gather x1, waiting for transfers between devices, on_device(): lax.all_gather(w_gate, 'req', axis=0, tiled=True)  51.6 us
    all_gather x1, waiting for transfers between devices, on_device(): lax.all_gather(w_up, 'req', axis=0, tiled=True)  43.5 us
    reduce_scatter x1, waiting for transfers between devices, on_device(): lax.psum_scatter(terms.astype(jnp.bfloat16), 'mp', scatter_dimension=1, t...  33.9 us
    all_gather x1, waiting for transfers between devices, on_device(): mid_full = lax.all_gather(mid_local, 'mp', axis=1, tiled=True)  32.8 us
    all_gather x1, waiting for transfers between devices, on_device(): full_rows = lax.all_gather(hidden_in, 'mp', axis=1, tiled=True)  27.4 us
  transfers between devices with their start and end apart: 9, of which 9 were waited for; matrix products, arithmetic and copies ran while one was open for 12% of the time, Pallas kernels for 0%

commit v1 on v0

--- a/solution.py
+++ b/solution.py
@@ -107,7 +107,17 @@
         preferred_element_type=jnp.float32,
     )
     upper = jnp.dot(
-        columns, lax.all_gather(w_up, "req", axis=0, tiled=True), preferred_element_type=jnp.float32
+        columns,
+        jnp.concatenate(
+            lax.all_to_all(
+                jnp.stack([w_up for _ in range(lax.psum(1, axis_name="req"))], axis=0),
+                axis_name="req",
+                split_axis=0,
+                concat_axis=0,
+            ),
+            axis=0,
+        ),
+        preferred_element_type=jnp.float32,
     )
     units = (jax.nn.silu(gate) * upper).astype(jnp.bfloat16)
     terms = jnp.dot(

time: 500 us -> 462 us (0.924)
  waiting for transfers between devices: 398 us -> 350 us
  starting transfers between devices: 0.57 us -> 7.72 us
    all_gather x1 -> x0, waiting for transfers between devices: 43.5 us -> none  [on_device(): lax.all_gather(w_up, 'req', axis=0, tiled=True)]
    all_gather x1, waiting for transfers between devices: 51.6 us -> 66.7 us  [on_device(): lax.all_gather(w_gate, 'req', axis=0, tiled=True)]
    all_gather x1, waiting for transfers between devices: 59.4 us -> 49.5 us  [on_device(): lax.all_gather(w_down, 'req', axis=1, tiled=True)]
    all_gather x1, waiting for transfers between devices: 32.8 us -> 23.9 us  [on_device(): mid_full = lax.all_gather(mid_local, 'mp', axis=1, tiled=True)]
    all_to_all x0 -> x1, starting transfers between devices: none -> 7.18 us  [on_device(): lax.all_to_all(jnp.stack([w_up for _ in range(lax.psum(1, axis_name='req'...]
    unnamed x15 -> x17, local copies, waits for them, and re-layouts: 12.2 us -> 12.3 us
  transfers between devices with their start and end apart: 9 -> 9, of which waited for: 9 -> 8; matrix products, arithmetic and copies ran while one was open for 12% -> 14% of each run, Pallas kernels for 0% -> 0%
where the time goes in v1:
time: 462 us; the launch traced here: 461 us
  waiting for transfers between devices  350 us (76%)
  matrix products  50 us (11%)
  other arithmetic  21.9 us (5%)
  local copies, waits for them, and re-layouts  16.3 us (4%)
  between operations  15 us (3%)
  starting transfers between devices  7.72 us (2%)
    reduce_scatter x1, waiting for transfers between devices, on_device(): lax.psum_scatter(partial_value.astype(jnp.bfloat16), 'mp', scatter_dimens...  79 us
    all_gather x1, waiting for transfers between devices, on_device(): lax.all_gather(w_gate, 'req', axis=0, tiled=True)  66.7 us
    all_gather x1, waiting for transfers between devices, on_device(): lax.all_gather(w_qkv, 'req', axis=1, tiled=True)  53.4 us
    all_gather x1, waiting for transfers between devices, on_device(): lax.all_gather(w_down, 'req', axis=1, tiled=True)  49.5 us
    reduce_scatter x1, waiting for transfers between devices, on_device(): lax.psum_scatter(terms.astype(jnp.bfloat16), 'mp', scatter_dimension=1, t...  33.9 us
    all_gather x1, waiting for transfers between devices, on_device(): full_rows = lax.all_gather(hidden_in, 'mp', axis=1, tiled=True)  27.4 us
    all_gather x1, waiting for transfers between devices, on_device(): mid_full = lax.all_gather(mid_local, 'mp', axis=1, tiled=True)  23.9 us
    dot_general x1, matrix products, on_device(): jnp.dot(units, lax.all_gather(w_down, 'req', axis=1, tiled=True), preferr...  15.3 us
  transfers between devices with their start and end apart: 9, of which 8 were waited for; matrix products, arithmetic and copies ran while one was open for 14% of the time, Pallas kernels for 0%

profile of v1, /device:TPU:0, one launch (start us, length us, event | category | flops | bytes accessed | tf_op | source)
XLA Modules:
  0.0 461.0 jit_solution(3620857353326705385)
XLA Ops:
  7.2 0.0 all-gather.7.cloned.1.call-start
  7.2 0.7 all-gather.7.cloned.1.call-update
  7.9 0.0 all-gather.9.cloned.1.call-start
  7.9 1.7 copy.15
  9.7 0.0 all-gather.9.cloned.1.call-update
  9.7 0.0 all-gather.11.cloned.1.call-start
  9.8 0.7 all-gather.11.cloned.1.call-update
  10.4 0.0 reduce-scatter.3.cloned.1.call-start
  10.5 1.3 iota_compare_fusion
  12.4 0.7 convert_element_type.87
  13.1 2.9 copy.17
  16.1 4.2 copy.18
  20.2 0.5 multiply_cosine_fusion
  20.8 27.4 %all-gather.7.cloned.1.call-done = bf16[1024,2048]{1,0:T(8,128)(2,1)} async-done(((bf16[1024,256]{1,0:T(8,128)(2,1)}), bf16[1024,2048]{1,0:T(8,128)(2,1)}) %all-gather.7.cloned.1.call-update) | async-done | bytes 4194320 | tf_op jit(solution)/shard_map/all_gather | solution.py:54
  48.2 3.1 fusion.23
  51.3 53.4 %all-gather.9.cloned.1.call-done = bf16[3,2048,256]{1,2,0:T(8,128)(2,1)} async-done(((bf16[3,128,256]{1,2,0:T(8,128)(2,1)}), bf16[3,2048,256]{1,2,0:T(8,128)(2,1)}) %all-gather.9.cloned.1.call-update) | async-done | bytes 3145744 | tf_op jit(solution)/shard_map/all_gather | solution.py:60
  104.7 6.6 %fusion.37 = f32[3,1024,256]{1,2,0:T(8,128)S(1)} fusion(bf16[3,2048,256]{1,2,0:T(8,128)(2,1)} %all-gather.9.cloned.1.call-done, bf16[1024,2048]{1,0:T(8,128)(2,1)} %all-gather.7.cloned.1.call-done, f32[2048]{0:T(1024)S(1)} %convert_element_type.87, f32[1024]{0:T(1024)S(1)} %add_rsqrt_fusion.1), kind=kOutput, calls=%fused_computation.49 | convolution fusion | flops 3229614080 | bytes 10498048 | tf_op jit(solution)/shard_map/nd,kdw->knw/dot_general | solution.py:57
  111.3 0.0 copy-start.2
  111.3 0.0 copy-start.1
  111.3 0.1 fusion.54
  111.5 0.1 slice.44
  111.5 0.2 subtract_convert_fusion
  111.7 0.2 multiply_subtract_fusion
  111.9 1.1 copy-done.2
  113.0 0.3 copy-done.1
  113.3 3.0 fusion.20
  116.4 4.2 fusion.22
  120.6 5.9 %fusion.40 = f32[4,1024,64]{1,2,0:T(8,128)} fusion(bf16[1024,4,64]{0,2,1:T(8,128)(2,1)S(1)} %bitcast.81, f32[4,1024,1024]{1,2,0:T(8,128)S(1)} %get-tuple-element.91, f32[4,1024]{1,0:T(4,128)S(1)} %get-tuple-element.87, pred[1024,1024]{0,1:T(8,128)(4,1)S(1)} %copy-done.1, f32[4,1024]{1,0:T(4,128)S(1)} %get-tuple-element.85), kind=kOutput, calls=%fused_computation.50 | convolution fusion | flops 558104576 | bytes 19431424 | tf_op jit(solution)/shard_map/hqk,khd->hqd/dot_general | solution.py:41
  126.5 8.1 %while.14 = (s32[]{:T(128)}, f32[4,1024,1]{1,0,2:T(4,128)S(1)}, f32[4,1024,1]{1,0,2:T(4,128)S(1)}, f32[4,1024,64]{1,2,0:T(8,128)}, s32[]{:T(128)}, /*index=5*/s3...) while((s32[]{:T(128)}, f32[4,1024,1]{1,0,2:T(4,128)S(1)}, ...), condition=%wide.region_6.7_spmd, body=%wide.region_3.6_spmd.sunk | while | flops 564671488 | bytes 36965104 | solution.py:92
  126.5 0.7 add_compare_fusion.2
  127.3 1.6 bitcast_reduce_fusion.2
  128.9 3.1 fusion.74
  132.0 2.5 fusion.73
  134.6 0.0 copy-start.3
  134.6 0.0 copy-start.6
  134.6 1.4 divide_convert_fusion
  136.0 13.5 %all-gather.11.cloned.1.call-done = bf16[256,2048]{1,0:T(8,128)(2,1)} async-done(((bf16[256,128]{1,0:T(8,128)(2,1)}), bf16[256,2048]{1,0:T(8,128)(2,1)}) %all-gather.11.cloned.1.call-update) | async-done | bytes 1048592 | tf_op jit(solution)/shard_map/all_gather | solution.py:95
  149.5 4.5 convolution_convert_fusion
  154.0 0.0 reduce-scatter.3.cloned.1.call-update
  154.0 0.0 copy-start.7
  154.0 0.0 all-gather.13.cloned.1.call-start
  154.1 79.0 %reduce-scatter.3.cloned.1.call-done = bf16[1024,256]{1,0:T(8,128)(2,1)} async-done(((bf16[1024,2048]{1,0:T(8,128)(2,1)}), bf16[1024,256]{1,0:T(8,128)(2,1)}) %reduce-scatter.3.cloned.1.call-update) | async-done | bytes 524304 | tf_op jit(solution)/shard_map/reduce_scatter | solution.py:97
  233.1 2.0 add_convert_fusion.1
  235.1 0.0 all-gather.13.cloned.1.call-update
  235.1 0.0 all-gather.15.cloned.1.call-start
  235.2 0.5 all-gather.15.cloned.1.call-update
  235.7 0.0 all-gather.17.cloned.1.call-start
  235.7 0.7 all-gather.17.cloned.1.call-update
  236.5 2.5 stack.2
  239.0 7.2 %all-to-all-start = ((bf16[16,128,1024]{2,1,0:T(8,128)(2,1)}), bf16[16,128,1024]{2,1,0:T(8,128)(2,1)}, u32[]{:S(2)}, u32[]{:S(2)}) async-start(bf16[16,128,1024]{2,1,0:T(8,128)(2,1)} %stack.2), calls=%async_computation.1 | async-start | bytes 8388608 | tf_op jit(solution)/shard_map/all_to_all | solution.py:112
  246.2 0.3 reduce-scatter.5.cloned.1.call-start
  246.5 23.9 %all-gather.13.cloned.1.call-done = bf16[1024,2048]{1,0:T(8,128)(2,1)} async-done(((bf16[1024,256]{1,0:T(8,128)(2,1)}), bf16[1024,2048]{1,0:T(8,128)(2,1)}) %all-gather.13.cloned.1.call-update) | async-done | bytes 4194320 | tf_op jit(solution)/shard_map/all_gather | solution.py:101
  270.4 3.1 fusion.26
  273.4 66.7 %all-gather.15.cloned.1.call-done = bf16[2048,1024]{1,0:T(8,128)(2,1)} async-done(((bf16[128,1024]{1,0:T(8,128)(2,1)}), bf16[2048,1024]{1,0:T(8,128)(2,1)}) %all-gather.15.cloned.1.call-update) | async-done | bytes 4194320 | tf_op jit(solution)/shard_map/all_gather | solution.py:106
  340.2 9.9 %fusion.44 = f32[1024,1024]{1,0:T(8,128)} fusion(bf16[2048,1024]{1,0:T(8,128)(2,1)} %all-gather.15.cloned.1.call-done, bf16[1024,2048]{1,0:T(8,128)(2,1)} %all-gather.13.cloned.1.call-done, f32[2048]{0:T(1024)S(1)} %convert_element_type.102, f32[1024]{0:T(1024)S(1)} %add_rsqrt_fusion), kind=kOutput, calls=%fused_computation.51 | convolution fusion | flops 4303355904 | bytes 12595200 | tf_op jit(solution)/shard_map/dot_general | solution.py:104
  350.1 0.0 all-to-all-done
  350.1 49.5 %all-gather.17.cloned.1.call-done = bf16[1024,2048]{1,0:T(8,128)(2,1)} async-done(((bf16[1024,128]{1,0:T(8,128)(2,1)}), bf16[1024,2048]{1,0:T(8,128)(2,1)}) %all-gather.17.cloned.1.call-update) | async-done | bytes 4194320 | tf_op jit(solution)/shard_map/all_gather | solution.py:124
  399.6 15.3 %convolution_convert_fusion.1 = bf16[1024,2048]{1,0:T(8,128)(2,1)} fusion(bf16[1024,2048]{1,0:T(8,128)(2,1)} %all-gather.17.cloned.1.call-done, f32[1024,1024]{1,0:T(8,128)} %fusion.44, bf16[2048,1024]{1,0:T(8,128)(2,1)} %bitcast.18, bf16[1024,2048]{1,0:T(8,128)(2,1)} %all-gather.13.cloned.1.call-done, f32[2048]{0:T(1024)S(1)} %convert_element_type.102, ...), kind=kOutput, calls=%fused_computation.48 | convolution fusion | flops 8606711808 | bytes 20983808 | tf_op jit(solution)/shard_map/dot_general | solution.py:123
  415.0 0.0 reduce-scatter.5.cloned.1.call-update
  415.0 1.0 copy.19
  416.0 1.3 slice_bitcast_fusion
  417.3 1.0 copy.20
  418.3 33.9 %reduce-scatter.5.cloned.1.call-done = bf16[1024,256]{1,0:T(8,128)(2,1)} async-done(((bf16[1024,2048]{1,0:T(8,128)(2,1)}), bf16[1024,256]{1,0:T(8,128)(2,1)}) %reduce-scatter.5.cloned.1.call-update) | async-done | bytes 524304 | tf_op jit(solution)/shard_map/reduce_scatter | solution.py:126
  452.2 2.0 add_convert_fusion
  (21 shorter events, 0.2 us)
Async XLA Ops:
  7.2 41.0 %all-gather.7.cloned.1.call-start = ((), (), s32[]{:S(2)}) async-start(), calls=%async_computation.3 | async-start | bytes 4718592 | tf_op jit(solution)/shard_map/all_gather | solution.py:54
  7.9 96.8 %all-gather.9.cloned.1.call-start = ((), (), s32[]{:S(2)}) async-start(), calls=%async_computation.4 | async-start | bytes 3342336 | tf_op jit(solution)/shard_map/all_gather | solution.py:60
  9.7 139.8 %all-gather.11.cloned.1.call-start = ((), (), s32[]{:S(2)}) async-start(), calls=%async_computation.5 | async-start | bytes 1114112 | tf_op jit(solution)/shard_map/all_gather | solution.py:95
  10.4 222.7 %reduce-scatter.3.cloned.1.call-start = ((), (), s32[]{:S(2)}) async-start(), calls=%async_computation.6 | async-start | bytes 4718592 | tf_op jit(solution)/shard_map/reduce_scatter | solution.py:97
  111.3 1.7 copy-start.2
  111.3 2.0 copy-start.1
  126.5 2.4 copy-start.4
  132.0 2.6 copy-start.5
  134.6 98.5 %copy-start.3 = (bf16[1024,256]{1,0:T(8,128)(2,1)S(1)}, bf16[1024,256]{1,0:T(8,128)(2,1)}, u32[]{:S(2)}) copy-start(bf16[1024,256]{1,0:T(8,128)(2,1)} %param.13) | copy-start | bytes 1572868
  134.6 101.8 %copy-start.6 = (bf16[128,1024]{1,0:T(8,128)(2,1)S(1)}, bf16[128,1024]{1,0:T(8,128)(2,1)}, u32[]{:S(2)}) copy-start(bf16[128,1024]{1,0:T(8,128)(2,1)} %param.19) | copy-start | bytes 786436
  154.0 92.4 %copy-start.7 = (bf16[2048]{0:T(1024)(128)(2,1)S(1)}, bf16[2048]{0:T(1024)(128)(2,1)}, u32[]{:S(2)}) copy-start(bf16[2048]{0:T(1024)(128)(2,1)} %param.17) | copy-start | bytes 12292
  154.0 116.3 %all-gather.13.cloned.1.call-start = ((), (), s32[]{:S(2)}) async-start(), calls=%async_computation.7 | async-start | bytes 4718592 | tf_op jit(solution)/shard_map/all_gather | solution.py:101
  235.1 105.1 %all-gather.15.cloned.1.call-start = ((), (), s32[]{:S(2)}) async-start(), calls=%async_computation.8 | async-start | bytes 4456448 | tf_op jit(solution)/shard_map/all_gather | solution.py:106
  235.7 163.9 %all-gather.17.cloned.1.call-start = ((), (), s32[]{:S(2)}) async-start(), calls=%async_computation.9 | async-start | bytes 4456448 | tf_op jit(solution)/shard_map/all_gather | solution.py:124
  239.0 111.1 %all-to-all-start = ((bf16[16,128,1024]{2,1,0:T(8,128)(2,1)}), bf16[16,128,1024]{2,1,0:T(8,128)(2,1)}, u32[]{:S(2)}, u32[]{:S(2)}) async-start(bf16[16,128,1024]{2,1,0:T(8,128)(2,1)} %stack.2), calls=%async_computation.1 | async-start | bytes 8388608 | tf_op jit(solution)/shard_map/all_to_all | solution.py:112
  246.2 206.0 %reduce-scatter.5.cloned.1.call-start = ((), (), s32[]{:S(2)}) async-start(), calls=%async_computation.10 | async-start | bytes 4718592 | tf_op jit(solution)/shard_map/reduce_scatter | solution.py:126
  415.0 37.2 %copy-start = (bf16[1024,256]{1,0:T(8,128)(2,1)S(1)}, bf16[1024,256]{1,0:T(8,128)(2,1)}, u32[]{:S(2)}) copy-start(bf16[1024,256]{1,0:T(8,128)(2,1)} %add_convert_fusion.1) | copy-start | bytes 1572868
Sparse Core Ops, SparseCore 0:
  9.7 38.4 all-gather.6
  50.9 53.7 all-gather.8
  106.8 42.7 all-gather.10
  154.2 78.9 reduce-scatter.2
  235.2 35.0 all-gather.12
  272.4 67.7 all-gather.14
  342.3 57.2 all-gather.16
  415.1 37.0 reduce-scatter.4
